TPU v7x, 256 devices: a whole 4x4x8 slice. The times are simulated.
256 devices in a mesh: pair: 32 (over z, x_lo, core), grp: 8 (over y, x_hi).
Axes of the slice: x: 4 (x_hi: 2, x_lo: 2; x = x_hi * 2 + x_lo), y: 4, z: 8, core: 2. Of those that a mesh axis runs over, the one named last changes fastest.
Arguments:
- amplitudes: float32 [8, 224, 2048], P('grp', 'pair'), may hold values from -6 to 6
- integrals: float32 [2048, 65536], P('grp', 'pair'), may hold values from -0.375 to 0.375
- owner_blocks: int32 [16], replicated, may hold values from 0 to 15, each once
- occ_pairs: int32 [8, 2, 224], P('grp'), may hold values from 0 to 63, as said below
- vir_pairs: int32 [2, 65536], replicated, may hold values from 0 to 511, as said below
- occ_energy: float32 [64], replicated, may hold values from -1.5 to -0.5
- vir_energy: float32 [512], replicated, may hold values from 0.2 to 1.5
Outputs:
- ladder: float32 [8, 224, 65536], P('grp', 'pair')
Inputs may be any that keep to these rules, and one draw needn't show every extreme that they name: `occ_pairs`: each column is a pair i<j; no pair occurs twice. `vir_pairs`: each column is a pair a<b; no pair occurs twice. `owner_blocks`: a permutation.
All inputs are finite; a program needn't handle non-finite values.
Results may differ from a plain program's by a relative error of at most 0.000071.
Values sent between devices are 32-bit elements; how exact they have to be, the bound alone decides.
No kernel may reach another device: no remote copies, remote signals or barrier semaphores. Data moves between devices by JAX's collectives and lax.ppermute only.
A program may use at most 64 MiB of HBM per device.

v0:
```python
import jax
import jax.numpy as jnp
import numpy as np
from jax import lax
from jax.sharding import Mesh, PartitionSpec as P

N_CHUNK = 4


def pair_energies(energy, pairs):
    return jnp.take(energy, pairs[0]) + jnp.take(energy, pairs[1])


def on_device(amplitudes, integrals, owner_blocks, occ_pairs, vir_pairs, occ_energy, vir_energy):
    rows_l = amplitudes.shape[1]
    width = amplitudes.shape[2]
    block = integrals.shape[0]
    columns = integrals.shape[1]
    nblocks = owner_blocks.shape[0]
    sub = width // nblocks
    per_block = block // sub
    ny = lax.axis_size("gy")
    nx = lax.axis_size("gx")
    npair = lax.axis_size("pair")
    gx = lax.axis_index("gx")
    p = lax.axis_index("pair")

    def half_blocks(x):
        m = jnp.arange(ny * per_block, dtype=jnp.int32)
        b = (m // per_block * nx + x) * per_block + m % per_block
        return jnp.take(owner_blocks, b)

    tau = amplitudes[0].reshape(rows_l, nblocks, sub)

    def select(x):
        return jnp.take(tau, half_blocks(x), axis=1).reshape(rows_l, -1)

    mine = select(gx)
    other = select(1 - gx)
    swap = [(0, 1), (1, 0)]
    got = lax.ppermute(other, "gx", swap)
    both = jnp.where(gx == 0, jnp.stack([mine, got]), jnp.stack([got, mine]))
    spread = jnp.broadcast_to(both[None], (npair,) + both.shape)
    t_all = lax.all_to_all(spread, "pair", 0, 0, tiled=True)
    lhs = t_all.reshape(npair * nx * rows_l, -1)
    occ_sum = pair_energies(occ_energy, occ_pairs[0]).reshape(npair, rows_l)
    vir_local = lax.dynamic_slice_in_dim(vir_pairs, p * columns, columns, 1)
    vir_sum = pair_energies(vir_energy, vir_local)
    w = columns // N_CHUNK
    outs = []
    for c in range(N_CHUNK):
        piece = lax.all_gather(integrals[:, c * w : (c + 1) * w], "gy", axis=0, tiled=True)
        part = jnp.dot(
            lhs, piece, precision=lax.Precision.HIGHEST, preferred_element_type=jnp.float32
        )
        part = part.reshape(npair, nx, rows_l, w)
        keep = lax.dynamic_index_in_dim(part, gx, 1, keepdims=False)
        send = lax.dynamic_index_in_dim(part, 1 - gx, 1, keepdims=False)
        work = keep + lax.ppermute(send, "gx", swap)
        payload = work / (occ_sum[:, :, None] - vir_sum[None, None, c * w : (c + 1) * w])
        outs.append(lax.all_to_all(payload, "pair", 0, 0, tiled=True))
    res = jnp.stack(outs, axis=2)
    res = jnp.transpose(res, (1, 0, 2, 3)).reshape(1, rows_l, npair * columns)
    return res


def solution(mesh):
    devs = np.asarray(mesh.devices)
    npair, ngrp = devs.shape
    nx = 2
    sub_mesh = Mesh(devs.reshape(npair, ngrp // nx, nx), ("pair", "gy", "gx"))
    g = ("gy", "gx")
    return jax.shard_map(
        on_device,
        mesh=sub_mesh,
        in_specs=(P(g, "pair", None), P(g, "pair"), P(), P(g, None, None), P(), P(), P()),
        out_specs=P(g, "pair", None),
        check_vma=False,
    )
```

profile of v0, /device:TPU:2, one launch (start us, length us, event | category | flops | bytes accessed | tf_op | source)
XLA Modules:
  0.0 309.0 jit_solution(17155572473532148239)
XLA Ops:
  6.5 3.0 fusion.20
  9.5 0.0 all-gather.9.cloned.1.call-update
  9.5 0.0 all-gather.11.cloned.1.call-start
  9.6 0.7 all-gather.11.cloned.1.call-update
  10.3 0.0 all-gather.7.cloned.1.call-start
  10.3 0.7 all-gather.7.cloned.1.call-update
  11.1 0.6 gather_fusion.2
  11.8 0.6 gather_fusion.3
  12.4 0.1 select_bitcast_fusion
  12.4 2.2 collective-permute-start
  14.6 0.6 gather_fusion
  15.3 0.6 gather_fusion.1
  15.9 0.1 select_bitcast_fusion.1
  15.9 2.0 collective-permute-done
  18.0 1.7 broadcast_in_dim.34
  19.7 10.2 %all-to-all-start = ((f32[32,2,7,1024]{3,1,2,0:T(2,128)}), f32[32,2,7,1024]{3,1,2,0:T(2,128)S(1)}, u32[]{:S(2)}, u32[]{:S(2)}) async-start(f32[32,2,7,1024]{3,1,2,0:T(2,128)} %broadcast_in_dim.34), calls=%async_computation | async-start | bytes 3670016 | tf_op jit(solution)/shard_map/all_to_all | solution.py:44
  29.9 0.0 all-gather.5.cloned.1.call-start
  29.9 0.5 all-gather.5.cloned.1.call-update
  30.5 1.9 gather_fusion.5
  32.4 2.0 gather_fusion.4
  34.5 0.9 constant_dynamic-slice_fusion
  35.4 10.6 %all-gather.9.cloned.1.call-done = f32[1024,512]{1,0:T(8,128)} async-done(((f32[256,512]{1,0:T(8,128)}), f32[1024,512]{1,0:T(8,128)}) %all-gather.9.cloned.1.call-update) | async-done | bytes 2097168 | tf_op jit(solution)/shard_map/all_gather | solution.py:52
  46.0 28.6 %all-to-all-done = f32[32,2,7,1024]{3,1,2,0:T(2,128)S(1)} async-done(((f32[32,2,7,1024]{3,1,2,0:T(2,128)}), f32[32,2,7,1024]{3,1,2,0:T(2,128)S(1)}, u32[]{:S(2)}, u32[]{:S(2)}) %all-to-all-start) | async-done | bytes 1835040 | tf_op jit(solution)/shard_map/all_to_all | solution.py:44
  74.6 5.2 %fusion.2 = f32[32,2,7,512]{3,0,2,1:T(8,128)S(1)} fusion(f32[1024,512]{1,0:T(8,128)} %all-gather.9.cloned.1.call-done, f32[32,2,7,1024]{3,1,2,0:T(2,128)S(1)} %all-to-all-done), kind=kOutput, calls=%fused_computation.11 | convolution fusion | flops 2818572288 | bytes 4849664 | tf_op jit(solution)/shard_map/dot_general | solution.py:53
  79.8 0.8 dynamic-slice_bitcast_fusion.1
  80.6 0.6 all-gather.11.cloned.1.call-done
  81.2 5.2 %fusion = f32[32,2,7,512]{3,0,2,1:T(8,128)S(1)} fusion(f32[1024,512]{1,0:T(8,128)} %all-gather.11.cloned.1.call-done, f32[32,2,7,1024]{3,1,2,0:T(2,128)S(1)} %all-to-all-done), kind=kOutput, calls=%fused_computation.9 | convolution fusion | flops 2818572288 | bytes 4849664 | tf_op jit(solution)/shard_map/dot_general | solution.py:53
  86.4 0.9 copy-done.3
  87.4 0.8 dynamic-slice_bitcast_fusion
  88.2 28.2 %all-gather.7.cloned.1.call-done = f32[1024,512]{1,0:T(8,128)} async-done(((f32[256,512]{1,0:T(8,128)}), f32[1024,512]{1,0:T(8,128)}) %all-gather.7.cloned.1.call-update) | async-done | bytes 2097168 | tf_op jit(solution)/shard_map/all_gather | solution.py:52
  116.4 5.2 %fusion.4 = f32[32,2,7,512]{3,0,2,1:T(8,128)S(1)} fusion(f32[1024,512]{1,0:T(8,128)} %all-gather.7.cloned.1.call-done, f32[32,2,7,1024]{3,1,2,0:T(2,128)S(1)} %all-to-all-done), kind=kOutput, calls=%fused_computation.13 | convolution fusion | flops 2818572288 | bytes 4849664 | tf_op jit(solution)/shard_map/dot_general | solution.py:53
  121.6 0.9 copy-done.5
  122.6 0.8 dynamic-slice_bitcast_fusion.2
  123.4 28.1 %all-gather.5.cloned.1.call-done = f32[1024,512]{1,0:T(8,128)} async-done(((f32[256,512]{1,0:T(8,128)}), f32[1024,512]{1,0:T(8,128)}) %all-gather.5.cloned.1.call-update) | async-done | bytes 2097168 | tf_op jit(solution)/shard_map/all_gather | solution.py:52
  151.5 5.4 %fusion.6 = f32[32,2,7,512]{3,0,2,1:T(8,128)S(1)} fusion(f32[1024,512]{1,0:T(8,128)} %all-gather.5.cloned.1.call-done, f32[32,2,7,1024]{3,1,2,0:T(2,128)S(1)} %all-to-all-done), kind=kOutput, calls=%fused_computation.15 | convolution fusion | flops 2818572288 | bytes 4849664 | tf_op jit(solution)/shard_map/dot_general | solution.py:53
  156.9 0.0 copy-start.7
  157.0 0.9 copy-done.7
  157.9 0.8 dynamic-slice_bitcast_fusion.3
  158.7 2.1 collective-permute-start.1
  160.7 1.4 collective-permute-start.2
  162.2 2.1 collective-permute-start.4
  164.3 1.4 collective-permute-start.3
  165.7 0.1 sub.31
  165.8 0.1 copy.44
  165.9 13.2 %gather_fusion.7 = f32[2048]{0:T(1024)S(1)} fusion(f32[512]{0:T(512)S(1)} %copy-done, s32[2048]{0:T(1024)S(1)} %fusion.17), kind=kCustom, calls=%fused_computation.7.clone | custom fusion | bytes 24576 | tf_op jit(solution)/shard_map/jit(_take)/gather | solution.py:11
  179.1 13.2 %gather_fusion.6 = f32[2048]{0:T(1024)S(1)} fusion(f32[512]{0:T(512)S(1)} %copy-done, s32[2048]{0:T(1024)S(1)} %fusion.16), kind=kCustom, calls=%fused_computation.3.clone | custom fusion | bytes 24576 | tf_op jit(solution)/shard_map/jit(_take)/gather | solution.py:11
  192.4 0.0 collective-permute-done.2
  192.4 1.1 collective-permute-done.4
  193.5 8.5 %collective-permute-done.3 = f32[32,7,512]{2,0,1:T(8,128)} collective-permute-done((f32[32,7,512]{2,0,1:T(8,128)}, f32[32,7,512]{2,0,1:T(8,128)}, u32[]{:S(2)}, u32[]{:S(2)}) %collective-permute-start.3) | collective-permute-done | bytes 458784 | tf_op jit(solution)/shard_map/ppermute | solution.py:59
  202.1 3.0 fusion.15
  205.1 1.1 copy.45
  206.1 8.6 %all-to-all-start.1 = ((f32[32,7,512]{2,1,0:T(8,128)}), f32[32,7,512]{2,1,0:T(8,128)S(1)}, u32[]{:S(2)}, u32[]{:S(2)}) async-start(f32[32,7,512]{2,1,0:T(8,128)} %copy.45), calls=%async_computation.1 | async-start | bytes 1048576 | tf_op jit(solution)/shard_map/all_to_all | solution.py:61
  214.8 1.1 copy.51
  215.8 16.6 %all-to-all-done.1 = f32[32,7,512]{2,1,0:T(8,128)S(1)} async-done(((f32[32,7,512]{2,1,0:T(8,128)}), f32[32,7,512]{2,1,0:T(8,128)S(1)}, u32[]{:S(2)}, u32[]{:S(2)}) %all-to-all-start.1) | async-done | bytes 458784 | tf_op jit(solution)/shard_map/all_to_all | solution.py:61
  232.4 3.8 %all-to-all-start.4 = ((f32[32,7,512]{2,1,0:T(8,128)}), f32[32,7,512]{2,1,0:T(8,128)S(1)}, u32[]{:S(2)}, u32[]{:S(2)}) async-start(f32[32,7,512]{2,1,0:T(8,128)} %copy.51), calls=%async_computation.4 | async-start | bytes 1048576 | tf_op jit(solution)/shard_map/all_to_all | solution.py:61
  236.2 1.1 copy.49
  237.3 16.7 %all-to-all-done.4 = f32[32,7,512]{2,1,0:T(8,128)S(1)} async-done(((f32[32,7,512]{2,1,0:T(8,128)}), f32[32,7,512]{2,1,0:T(8,128)S(1)}, u32[]{:S(2)}, u32[]{:S(2)}) %all-to-all-start.4) | async-done | bytes 458784 | tf_op jit(solution)/shard_map/all_to_all | solution.py:61
  254.0 4.1 %all-to-all-start.3 = ((f32[32,7,512]{2,1,0:T(8,128)}), f32[32,7,512]{2,1,0:T(8,128)S(1)}, u32[]{:S(2)}, u32[]{:S(2)}) async-start(f32[32,7,512]{2,1,0:T(8,128)} %copy.49), calls=%async_computation.3 | async-start | bytes 1048576 | tf_op jit(solution)/shard_map/all_to_all | solution.py:61
  258.1 0.3 copy.47
  258.4 17.5 %all-to-all-done.3 = f32[32,7,512]{2,1,0:T(8,128)S(1)} async-done(((f32[32,7,512]{2,1,0:T(8,128)}), f32[32,7,512]{2,1,0:T(8,128)S(1)}, u32[]{:S(2)}, u32[]{:S(2)}) %all-to-all-start.3) | async-done | bytes 458784 | tf_op jit(solution)/shard_map/all_to_all | solution.py:61
  275.9 21.0 %all_to_all.25 = f32[32,7,512]{2,1,0:T(8,128)S(1)} all-to-all(f32[32,7,512]{2,1,0:T(8,128)S(1)} %copy.47), channel_id=1, replica_groups=mesh['pair'=32,'gy'=4,'gx'=2] {'pair'}, dimensions={0} | all-to-all | bytes 917504 | tf_op jit(solution)/shard_map/all_to_all | solution.py:61
  296.8 0.3 maximum_bitcast_fusion
  297.1 1.2 copy.52
  298.3 4.2 %reshape.175 = f32[1,7,65536]{2,0,1:T(1,128)} reshape(f32[7,32,4,512]{3,2,1,0:T(4,128)S(1)} %copy.52) | data formatting | bytes 3670016 | tf_op jit(solution)/shard_map/reshape | solution.py:63
  (43 shorter events, 0.3 us)
Async XLA Ops:
  6.5 159.4 %copy-start = (f32[512]{0:T(512)S(1)}, f32[512]{0:T(512)}, u32[]{:S(2)}) copy-start(f32[512]{0:T(512)} %param.21) | copy-start | bytes 6148
  6.5 4.5 %copy-start.11 = (f32[1,7,2048]{2,0,1:T(1,128)S(1)}, f32[1,7,2048]{2,0,1:T(1,128)}, u32[]{:S(2)}) copy-start(f32[1,7,2048]{2,0,1:T(1,128)} %param.15) | copy-start | bytes 172036
  6.5 4.6 %copy-start.2 = (s32[16]{0:T(128)S(1)}, s32[16]{0:T(128)}, u32[]{:S(2)}) copy-start(s32[16]{0:T(128)} %param.17) | copy-start | bytes 196
  6.5 39.4 %all-gather.9.cloned.1.call-start = ((), (), s32[]{:S(2)}) async-start(), calls=%async_computation.7 | async-start | bytes 2621440 | tf_op jit(solution)/shard_map/all_gather | solution.py:52
  9.5 71.7 %all-gather.11.cloned.1.call-start = ((), (), s32[]{:S(2)}) async-start(), calls=%async_computation.8 | async-start | bytes 2621440 | tf_op jit(solution)/shard_map/all_gather | solution.py:52
  10.3 106.1 %all-gather.7.cloned.1.call-start = ((), (), s32[]{:S(2)}) async-start(), calls=%async_computation.6 | async-start | bytes 2621440 | tf_op jit(solution)/shard_map/all_gather | solution.py:52
  12.4 5.5 %collective-permute-start = (f32[7,1024]{1,0:T(8,128)S(1)}, f32[7,1024]{1,0:T(8,128)S(1)}, u32[]{:S(2)}, u32[]{:S(2)}) collective-permute-start(f32[7,1024]{1,0:T(8,128)S(1)} %select_bitcast_fusion), channel_id=1, source_target_pairs={{0,1},{1,0},{2,3},{3,2},{4,5},{5,4},{6,7},{7,6},{8,9},{9,8},{10,11... | collective-permute-start | bytes 86024 | tf_op jit(solution)/shard_map/ppermute | solution.py:41
  19.7 10.8 %copy-start.12 = (s32[1,2,224]{2,1,0:T(2,128)S(1)}, s32[1,2,224]{2,1,0:T(2,128)}, u32[]{:S(2)}) copy-start(s32[1,2,224]{2,1,0:T(2,128)} %param.18) | copy-start | bytes 5380
  19.7 10.9 %copy-start.1 = (f32[64]{0:T(128)S(1)}, f32[64]{0:T(128)}, u32[]{:S(2)}) copy-start(f32[64]{0:T(128)} %param.20) | copy-start | bytes 772
  19.7 54.9 %all-to-all-start = ((f32[32,2,7,1024]{3,1,2,0:T(2,128)}), f32[32,2,7,1024]{3,1,2,0:T(2,128)S(1)}, u32[]{:S(2)}, u32[]{:S(2)}) async-start(f32[32,2,7,1024]{3,1,2,0:T(2,128)} %broadcast_in_dim.34), calls=%async_computation | async-start | bytes 3670016 | tf_op jit(solution)/shard_map/all_to_all | solution.py:44
  29.9 121.6 %all-gather.5.cloned.1.call-start = ((), (), s32[]{:S(2)}) async-start(), calls=%async_computation.5 | async-start | bytes 2621440 | tf_op jit(solution)/shard_map/all_gather | solution.py:52
  86.4 1.0 copy-start.3
  121.6 0.9 copy-start.5
  156.9 0.9 copy-start.7
  158.7 33.7 %collective-permute-start.1 = (f32[32,7,512]{2,0,1:T(8,128)}, f32[32,7,512]{2,0,1:T(8,128)S(1)}, u32[]{:S(2)}, u32[]{:S(2)}) collective-permute-start(f32[32,7,512]{2,0,1:T(8,128)} %dynamic-slice_bitcast_fusion.3), channel_id=1, source_target_pairs={{0,1},{1,0},{2,3},{3,2},{4,5},{5,4},{6,7},{7,6},{8,9},{9,8},{10,11... | collective-permute-start | bytes 1376264 | tf_op jit(solution)/shard_map/ppermute | solution.py:59
  160.7 31.6 %collective-permute-start.2 = (f32[32,7,512]{2,0,1:T(8,128)}, f32[32,7,512]{2,0,1:T(8,128)}, u32[]{:S(2)}, u32[]{:S(2)}) collective-permute-start(f32[32,7,512]{2,0,1:T(8,128)} %dynamic-slice_bitcast_fusion.2), channel_id=1, source_target_pairs={{0,1},{1,0},{2,3},{3,2},{4,5},{5,4},{6,7},{7,6},{8,9},{9,8},{10,11... | collective-permute-start | bytes 1376264 | tf_op jit(solution)/shard_map/ppermute | solution.py:59
  162.2 31.3 %collective-permute-start.4 = (f32[32,7,512]{2,0,1:T(8,128)}, f32[32,7,512]{2,0,1:T(8,128)}, u32[]{:S(2)}, u32[]{:S(2)}) collective-permute-start(f32[32,7,512]{2,0,1:T(8,128)} %dynamic-slice_bitcast_fusion), channel_id=1, source_target_pairs={{0,1},{1,0},{2,3},{3,2},{4,5},{5,4},{6,7},{7,6},{8,9},{9,8},{10,11... | collective-permute-start | bytes 1376264 | tf_op jit(solution)/shard_map/ppermute | solution.py:59
  164.3 37.8 %collective-permute-start.3 = (f32[32,7,512]{2,0,1:T(8,128)}, f32[32,7,512]{2,0,1:T(8,128)}, u32[]{:S(2)}, u32[]{:S(2)}) collective-permute-start(f32[32,7,512]{2,0,1:T(8,128)} %dynamic-slice_bitcast_fusion.1), channel_id=1, source_target_pairs={{0,1},{1,0},{2,3},{3,2},{4,5},{5,4},{6,7},{7,6},{8,9},{9,8},{10,11... | collective-permute-start | bytes 1376264 | tf_op jit(solution)/shard_map/ppermute | solution.py:59
  179.1 23.0 %copy-start.4 = (f32[32,2,7,512]{3,0,2,1:T(8,128)S(1)}, f32[32,2,7,512]{3,0,2,1:T(8,128)}, u32[]{:S(2)}) copy-start(f32[32,2,7,512]{3,0,2,1:T(8,128)} %copy-done.3) | copy-start | bytes 2752516
  179.1 22.9 %copy-start.6 = (f32[32,2,7,512]{3,0,2,1:T(8,128)S(1)}, f32[32,2,7,512]{3,0,2,1:T(8,128)}, u32[]{:S(2)}) copy-start(f32[32,2,7,512]{3,0,2,1:T(8,128)} %copy-done.5) | copy-start | bytes 2752516
  192.4 9.7 %copy-start.10 = (f32[32,7,512]{2,0,1:T(8,128)}, f32[32,7,512]{2,0,1:T(8,128)S(1)}, u32[]{:S(2)}) copy-start(f32[32,7,512]{2,0,1:T(8,128)S(1)} %collective-permute-done.1) | copy-start | bytes 1376260
  205.1 9.7 %copy-start.9 = (f32[32,7,512]{2,0,1:T(8,128)S(1)}, f32[32,7,512]{2,0,1:T(8,128)}, u32[]{:S(2)}) copy-start(f32[32,7,512]{2,0,1:T(8,128)} %get-tuple-element.24) | copy-start | bytes 1376260
  205.1 31.2 %copy-start.8 = (f32[32,7,512]{2,0,1:T(8,128)S(1)}, f32[32,7,512]{2,0,1:T(8,128)}, u32[]{:S(2)}) copy-start(f32[32,7,512]{2,0,1:T(8,128)} %get-tuple-element.25) | copy-start | bytes 1376260
  206.1 26.3 %all-to-all-start.1 = ((f32[32,7,512]{2,1,0:T(8,128)}), f32[32,7,512]{2,1,0:T(8,128)S(1)}, u32[]{:S(2)}, u32[]{:S(2)}) async-start(f32[32,7,512]{2,1,0:T(8,128)} %copy.45), calls=%async_computation.1 | async-start | bytes 1048576 | tf_op jit(solution)/shard_map/all_to_all | solution.py:61
  232.4 21.5 %all-to-all-start.4 = ((f32[32,7,512]{2,1,0:T(8,128)}), f32[32,7,512]{2,1,0:T(8,128)S(1)}, u32[]{:S(2)}, u32[]{:S(2)}) async-start(f32[32,7,512]{2,1,0:T(8,128)} %copy.51), calls=%async_computation.4 | async-start | bytes 1048576 | tf_op jit(solution)/shard_map/all_to_all | solution.py:61
  254.0 21.9 %all-to-all-start.3 = ((f32[32,7,512]{2,1,0:T(8,128)}), f32[32,7,512]{2,1,0:T(8,128)S(1)}, u32[]{:S(2)}, u32[]{:S(2)}) async-start(f32[32,7,512]{2,1,0:T(8,128)} %copy.49), calls=%async_computation.3 | async-start | bytes 1048576 | tf_op jit(solution)/shard_map/all_to_all | solution.py:61
Sparse Core Ops, SparseCore 0:
  9.7 36.2 all-gather.8
  47.8 33.3 all-gather.10
  83.0 33.3 all-gather.6
  118.1 33.3 all-gather.4
where the time goes:
time: 310 us; the launch traced here: 309 us
  waiting for transfers between devices  160 us (52%)
  local copies, waits for them, and re-layouts  53.5 us (17%)
  starting transfers between devices  36.1 us (12%)
  matrix products  21.1 us (7%)
  blocking collectives  21 us (7%)
  between operations  13.5 us (4%)
  other arithmetic  3.49 us (1%)
    all_gather x4, waiting for transfers between devices, on_device(): lax.all_gather(integrals[:, c * w:(c + 1) * w], 'gy', axis=0, tiled=True)  67.5 us
    all_to_all x3, waiting for transfers between devices, on_device(): outs.append(lax.all_to_all(payload, 'pair', 0, 0, tiled=True))  50.7 us
    gather x4, local copies, waits for them, and re-layouts, pair_energies(): return jnp.take(energy, pairs[0]) + jnp.take(energy, pairs[1])  30.3 us
    all_to_all x1, waiting for transfers between devices, on_device(): t_all = lax.all_to_all(spread, 'pair', 0, 0, tiled=True)  28.6 us
    dot_general x4, matrix products, on_device(): jnp.dot(lhs, piece, precision=lax.Precision.HIGHEST, preferred_element_ty...  21.1 us
    all_to_all x1, blocking collectives, on_device(): outs.append(lax.all_to_all(payload, 'pair', 0, 0, tiled=True))  21 us
    all_to_all x3, starting transfers between devices, on_device(): outs.append(lax.all_to_all(payload, 'pair', 0, 0, tiled=True))  16.5 us
    all_to_all x1, starting transfers between devices, on_device(): t_all = lax.all_to_all(spread, 'pair', 0, 0, tiled=True)  10.2 us
  transfers between devices with their start and end apart: 13, of which 11 were waited for; matrix products, arithmetic and copies ran while one was open for 18% of the time, Pallas kernels for 0%

commit v1 on v0

--- a/solution.py
+++ b/solution.py
@@ -49,7 +49,12 @@
     w = columns // N_CHUNK
     outs = []
     for c in range(N_CHUNK):
-        piece = lax.all_gather(integrals[:, c * w : (c + 1) * w], "gy", axis=0, tiled=True)
+        piece = jnp.concatenate(
+            lax.all_to_all(
+                jnp.stack([integrals[:, c * w : (c + 1) * w]] * lax.axis_size("gy")), "gy", 0, 0
+            ),
+            axis=0,
+        )
         part = jnp.dot(
             lhs, piece, precision=lax.Precision.HIGHEST, preferred_element_type=jnp.float32
         )

time: 310 us -> 320 us (1.032)
  blocking collectives: 21 us -> 51.7 us
  waiting for transfers between devices: 160 us -> 141 us
  between operations: 13.5 us -> 0.47 us
  starting transfers between devices: 36.1 us -> 44.9 us
  local copies, waits for them, and re-layouts: 53.5 us -> 59.3 us
  matrix products: 21.1 us -> 17.8 us
    all_gather x4 -> x0, waiting for transfers between devices: 67.5 us -> none  [on_device(): lax.all_gather(integrals[:, c * w:(c + 1) * w], 'gy', axis=0, tiled=True)]
    all_to_all x0 -> x3, waiting for transfers between devices: none -> 48.7 us  [on_device(): lax.all_to_all(jnp.stack([integrals[:, c * w:(c + 1) * w]] * lax.axis_siz...]
    all_to_all x0 -> x1, blocking collectives: none -> 30.7 us  [on_device(): lax.all_to_all(jnp.stack([integrals[:, c * w:(c + 1) * w]] * lax.axis_siz...]
    all_to_all x0 -> x3, starting transfers between devices: none -> 11.9 us  [on_device(): lax.all_to_all(jnp.stack([integrals[:, c * w:(c + 1) * w]] * lax.axis_siz...]
    all_to_all x1, waiting for transfers between devices: 28.6 us -> 39.9 us  [on_device(): t_all = lax.all_to_all(spread, 'pair', 0, 0, tiled=True)]
    ppermute x4, waiting for transfers between devices: 9.67 us -> 0.01 us  [on_device(): work = keep + lax.ppermute(send, 'gx', swap)]
    another operation x0 -> x4, local copies, waits for them, and re-layouts: none -> 5.08 us  [on_device(): jnp.stack([integrals[:, c * w:(c + 1) * w]] * lax.axis_size('gy'))]
    all_to_all x3, starting transfers between devices: 16.5 us -> 12.8 us  [on_device(): outs.append(lax.all_to_all(payload, 'pair', 0, 0, tiled=True))]
  transfers between devices with their start and end apart: 13 -> 12, of which waited for: 11 -> 8; matrix products, arithmetic and copies ran while one was open for 18% -> 18% of each run, Pallas kernels for 0% -> 0%
where the time goes in v1:
time: 320 us; the launch traced here: 319 us
  waiting for transfers between devices  141 us (44%)
  local copies, waits for them, and re-layouts  59.3 us (19%)
  blocking collectives  51.7 us (16%)
  starting transfers between devices  44.9 us (14%)
  matrix products  17.8 us (6%)
  other arithmetic  3.47 us (1%)
    all_to_all x3, waiting for transfers between devices, on_device(): outs.append(lax.all_to_all(payload, 'pair', 0, 0, tiled=True))  50.8 us
    all_to_all x3, waiting for transfers between devices, on_device(): lax.all_to_all(jnp.stack([integrals[:, c * w:(c + 1) * w]] * lax.axis_siz...  48.7 us
    all_to_all x1, waiting for transfers between devices, on_device(): t_all = lax.all_to_all(spread, 'pair', 0, 0, tiled=True)  39.9 us
    all_to_all x1, blocking collectives, on_device(): lax.all_to_all(jnp.stack([integrals[:, c * w:(c + 1) * w]] * lax.axis_siz...  30.7 us
    gather x4, local copies, waits for them, and re-layouts, pair_energies(): return jnp.take(energy, pairs[0]) + jnp.take(energy, pairs[1])  30.1 us
    all_to_all x1, blocking collectives, on_device(): outs.append(lax.all_to_all(payload, 'pair', 0, 0, tiled=True))  21 us
    dot_general x4, matrix products, on_device(): jnp.dot(lhs, piece, precision=lax.Precision.HIGHEST, preferred_element_ty...  17.8 us
    all_to_all x3, starting transfers between devices, on_device(): outs.append(lax.all_to_all(payload, 'pair', 0, 0, tiled=True))  12.8 us
  transfers between devices with their start and end apart: 12, of which 8 were waited for; matrix products, arithmetic and copies ran while one was open for 18% of the time, Pallas kernels for 0%

profile of v1, /device:TPU:2, one launch (start us, length us, event | category | flops | bytes accessed | tf_op | source)
XLA Modules:
  0.0 319.0 jit_solution(14531354503891401753)
XLA Ops:
  0.0 1.7 fusion.16
  1.7 0.3 stack.61
  2.0 30.7 %all_to_all.45 = f32[4,256,512]{2,1,0:T(8,128)} all-to-all(f32[4,256,512]{2,1,0:T(8,128)S(1)} %stack.61), channel_id=1, replica_groups=mesh['pair'=32,'gy'=4,'gx'=2] {'gy'}, dimensions={0} | all-to-all | bytes 4194304 | tf_op jit(solution)/shard_map/all_to_all | solution.py:53
  32.7 1.6 stack.63
  34.3 3.7 %all-to-all-start.5 = ((f32[4,256,512]{2,1,0:T(8,128)}), f32[4,256,512]{2,1,0:T(8,128)S(1)}, u32[]{:S(2)}, u32[]{:S(2)}) async-start(f32[4,256,512]{2,1,0:T(8,128)} %stack.63), calls=%async_computation.5 | async-start | bytes 4194304 | tf_op jit(solution)/shard_map/all_to_all | solution.py:53
  38.1 25.4 %all-to-all-done.5 = f32[4,256,512]{2,1,0:T(8,128)S(1)} async-done(((f32[4,256,512]{2,1,0:T(8,128)}), f32[4,256,512]{2,1,0:T(8,128)S(1)}, u32[]{:S(2)}, u32[]{:S(2)}) %all-to-all-start.5) | async-done | bytes 2097184 | tf_op jit(solution)/shard_map/all_to_all | solution.py:53
  63.5 1.3 copy-done.3
  64.8 1.6 stack.65
  66.4 3.7 %all-to-all-start.7 = ((f32[4,256,512]{2,1,0:T(8,128)}), f32[4,256,512]{2,1,0:T(8,128)S(1)}, u32[]{:S(2)}, u32[]{:S(2)}) async-start(f32[4,256,512]{2,1,0:T(8,128)} %stack.65), calls=%async_computation.7 | async-start | bytes 4194304 | tf_op jit(solution)/shard_map/all_to_all | solution.py:53
  70.2 0.6 gather_fusion.2
  70.9 0.6 gather_fusion.3
  71.5 0.1 select_bitcast_fusion
  71.5 2.2 collective-permute-start
  73.7 0.6 gather_fusion
  74.4 0.6 gather_fusion.1
  75.0 0.1 select_bitcast_fusion.1
  75.1 2.0 collective-permute-done
  77.1 17.7 %all-to-all-done.7 = f32[4,256,512]{2,1,0:T(8,128)S(1)} async-done(((f32[4,256,512]{2,1,0:T(8,128)}), f32[4,256,512]{2,1,0:T(8,128)S(1)}, u32[]{:S(2)}, u32[]{:S(2)}) %all-to-all-start.7) | async-done | bytes 2097184 | tf_op jit(solution)/shard_map/all_to_all | solution.py:53
  94.8 1.4 copy-done.5
  96.2 1.7 broadcast_in_dim.34
  97.9 10.2 %all-to-all-start = ((f32[32,2,7,1024]{3,1,2,0:T(2,128)}), f32[32,2,7,1024]{3,1,2,0:T(2,128)S(1)}, u32[]{:S(2)}, u32[]{:S(2)}) async-start(f32[32,2,7,1024]{3,1,2,0:T(2,128)} %broadcast_in_dim.34), calls=%async_computation | async-start | bytes 3670016 | tf_op jit(solution)/shard_map/all_to_all | solution.py:44
  108.2 1.9 gather_fusion.4
  110.0 1.9 gather_fusion.5
  111.9 0.9 constant_dynamic-slice_fusion
  112.8 39.9 %all-to-all-done = f32[32,2,7,1024]{3,1,2,0:T(2,128)S(1)} async-done(((f32[32,2,7,1024]{3,1,2,0:T(2,128)}), f32[32,2,7,1024]{3,1,2,0:T(2,128)S(1)}, u32[]{:S(2)}, u32[]{:S(2)}) %all-to-all-start) | async-done | bytes 1835040 | tf_op jit(solution)/shard_map/all_to_all | solution.py:44
  152.8 1.6 stack.59
  154.3 4.4 %all-to-all-start.1 = ((f32[4,256,512]{2,1,0:T(8,128)}), f32[4,256,512]{2,1,0:T(8,128)}, u32[]{:S(2)}, u32[]{:S(2)}) async-start(f32[4,256,512]{2,1,0:T(8,128)} %stack.59), calls=%async_computation.1 | async-start | bytes 4194304 | tf_op jit(solution)/shard_map/all_to_all | solution.py:53
  158.8 5.3 %fusion.4 = f32[32,2,7,512]{3,0,2,1:T(8,128)S(1)} fusion(f32[1024,512,1,1]{1,0,3,2:T(8,128)} %bitcast.69, f32[32,2,7,1024]{3,1,2,0:T(2,128)S(1)} %all-to-all-done), kind=kOutput, calls=%fused_computation.13 | convolution fusion | flops 2818572288 | bytes 4849664 | tf_op jit(solution)/shard_map/dot_general | solution.py:58
  164.2 0.9 dynamic-slice_bitcast_fusion.2
  165.1 2.1 collective-permute-start.2
  167.2 3.6 %fusion.2 = f32[32,2,7,512]{3,0,2,1:T(8,128)S(1)} fusion(f32[1024,512,1,1]{1,0,3,2:T(8,128)S(1)} %bitcast.68, f32[32,2,7,1024]{3,1,2,0:T(2,128)S(1)} %all-to-all-done), kind=kOutput, calls=%fused_computation.11 | convolution fusion | flops 2818572288 | bytes 4849664 | tf_op jit(solution)/shard_map/dot_general | solution.py:58
  170.8 1.0 dynamic-slice_bitcast_fusion.1
  171.8 1.4 collective-permute-start.3
  173.2 3.6 %fusion = f32[32,2,7,512]{3,0,2,1:T(8,128)S(1)} fusion(f32[1024,512,1,1]{1,0,3,2:T(8,128)S(1)} %bitcast.70, f32[32,2,7,1024]{3,1,2,0:T(2,128)S(1)} %all-to-all-done), kind=kOutput, calls=%fused_computation.9 | convolution fusion | flops 2818572288 | bytes 4849664 | tf_op jit(solution)/shard_map/dot_general | solution.py:58
  176.8 0.9 dynamic-slice_bitcast_fusion
  177.8 0.2 copy-done.9
  177.9 2.1 collective-permute-start.4
  180.1 5.6 %all-to-all-done.1 = f32[4,256,512]{2,1,0:T(8,128)} async-done(((f32[4,256,512]{2,1,0:T(8,128)}), f32[4,256,512]{2,1,0:T(8,128)}, u32[]{:S(2)}, u32[]{:S(2)}) %all-to-all-start.1) | async-done | bytes 2097184 | tf_op jit(solution)/shard_map/all_to_all | solution.py:53
  185.7 5.2 %fusion.6 = f32[32,2,7,512]{3,0,2,1:T(8,128)S(1)} fusion(f32[1024,512,1,1]{1,0,3,2:T(8,128)} %bitcast.9, f32[32,2,7,1024]{3,1,2,0:T(2,128)S(1)} %all-to-all-done), kind=kOutput, calls=%fused_computation.15 | convolution fusion | flops 2818572288 | bytes 4849664 | tf_op jit(solution)/shard_map/dot_general | solution.py:58
  190.9 0.0 copy-start.11
  190.9 0.9 copy-done.11
  191.8 0.8 dynamic-slice_bitcast_fusion.3
  192.6 2.1 collective-permute-start.1
  194.8 13.2 %gather_fusion.6 = f32[2048]{0:T(1024)S(1)} fusion(f32[512]{0:T(512)S(1)} %copy-done, s32[2048]{0:T(1024)S(1)} %fusion.12), kind=kCustom, calls=%fused_computation.3.clone | custom fusion | bytes 24576 | tf_op jit(solution)/shard_map/jit(_take)/gather | solution.py:11
  208.0 13.2 %gather_fusion.7 = f32[2048]{0:T(1024)S(1)} fusion(f32[512]{0:T(512)S(1)} %copy-done, s32[2048]{0:T(1024)S(1)} %fusion.13), kind=kCustom, calls=%fused_computation.7.clone | custom fusion | bytes 24576 | tf_op jit(solution)/shard_map/jit(_take)/gather | solution.py:11
  221.2 0.1 sub.31
  221.3 0.1 copy.44
  221.4 0.0 collective-permute-done.4
  221.4 0.8 copy-done.14
  222.2 2.9 fusion.11
  225.2 1.1 copy.45
  226.3 4.6 %all-to-all-start.2 = ((f32[32,7,512]{2,1,0:T(8,128)}), f32[32,7,512]{2,1,0:T(8,128)S(1)}, u32[]{:S(2)}, u32[]{:S(2)}) async-start(f32[32,7,512]{2,1,0:T(8,128)} %copy.45), calls=%async_computation.2 | async-start | bytes 1048576 | tf_op jit(solution)/shard_map/all_to_all | solution.py:66
  230.8 1.1 copy.47
  231.9 16.7 %all-to-all-done.2 = f32[32,7,512]{2,1,0:T(8,128)S(1)} async-done(((f32[32,7,512]{2,1,0:T(8,128)}), f32[32,7,512]{2,1,0:T(8,128)S(1)}, u32[]{:S(2)}, u32[]{:S(2)}) %all-to-all-start.2) | async-done | bytes 458784 | tf_op jit(solution)/shard_map/all_to_all | solution.py:66
  248.6 4.1 %all-to-all-start.4 = ((f32[32,7,512]{2,1,0:T(8,128)}), f32[32,7,512]{2,1,0:T(8,128)S(1)}, u32[]{:S(2)}, u32[]{:S(2)}) async-start(f32[32,7,512]{2,1,0:T(8,128)} %copy.47), calls=%async_computation.4 | async-start | bytes 1048576 | tf_op jit(solution)/shard_map/all_to_all | solution.py:66
  252.7 1.1 copy.49
  253.8 16.7 %all-to-all-done.4 = f32[32,7,512]{2,1,0:T(8,128)S(1)} async-done(((f32[32,7,512]{2,1,0:T(8,128)}), f32[32,7,512]{2,1,0:T(8,128)S(1)}, u32[]{:S(2)}, u32[]{:S(2)}) %all-to-all-start.4) | async-done | bytes 458784 | tf_op jit(solution)/shard_map/all_to_all | solution.py:66
  270.5 4.1 %all-to-all-start.6 = ((f32[32,7,512]{2,1,0:T(8,128)}), f32[32,7,512]{2,1,0:T(8,128)S(1)}, u32[]{:S(2)}, u32[]{:S(2)}) async-start(f32[32,7,512]{2,1,0:T(8,128)} %copy.49), calls=%async_computation.6 | async-start | bytes 1048576 | tf_op jit(solution)/shard_map/all_to_all | solution.py:66
  274.6 0.3 copy.51
  274.9 17.5 %all-to-all-done.6 = f32[32,7,512]{2,1,0:T(8,128)S(1)} async-done(((f32[32,7,512]{2,1,0:T(8,128)}), f32[32,7,512]{2,1,0:T(8,128)S(1)}, u32[]{:S(2)}, u32[]{:S(2)}) %all-to-all-start.6) | async-done | bytes 458784 | tf_op jit(solution)/shard_map/all_to_all | solution.py:66
  292.4 21.0 %all_to_all.46 = f32[32,7,512]{2,1,0:T(8,128)S(1)} all-to-all(f32[32,7,512]{2,1,0:T(8,128)S(1)} %copy.51), channel_id=1, replica_groups=mesh['pair'=32,'gy'=4,'gx'=2] {'pair'}, dimensions={0} | all-to-all | bytes 917504 | tf_op jit(solution)/shard_map/all_to_all | solution.py:66
  313.3 0.3 maximum_bitcast_fusion
  313.6 1.2 copy.52
  314.8 4.2 %reshape.199 = f32[1,7,65536]{2,0,1:T(1,128)} reshape(f32[7,32,4,512]{3,2,1,0:T(4,128)S(1)} %copy.52) | data formatting | bytes 3670016 | tf_op jit(solution)/shard_map/reshape | solution.py:68
  (50 shorter events, 0.3 us)
Async XLA Ops:
  0.0 194.8 %copy-start = (f32[512]{0:T(512)S(1)}, f32[512]{0:T(512)}, u32[]{:S(2)}) copy-start(f32[512]{0:T(512)} %param.21) | copy-start | bytes 6148
  34.3 3.8 %copy-start.15 = (f32[1,7,2048]{2,0,1:T(1,128)S(1)}, f32[1,7,2048]{2,0,1:T(1,128)}, u32[]{:S(2)}) copy-start(f32[1,7,2048]{2,0,1:T(1,128)} %param.15) | copy-start | bytes 172036
  34.3 29.2 %all-to-all-start.5 = ((f32[4,256,512]{2,1,0:T(8,128)}), f32[4,256,512]{2,1,0:T(8,128)S(1)}, u32[]{:S(2)}, u32[]{:S(2)}) async-start(f32[4,256,512]{2,1,0:T(8,128)} %stack.63), calls=%async_computation.5 | async-start | bytes 4194304 | tf_op jit(solution)/shard_map/all_to_all | solution.py:53
  63.5 1.3 copy-start.3
  66.4 3.8 %copy-start.2 = (s32[16]{0:T(128)S(1)}, s32[16]{0:T(128)}, u32[]{:S(2)}) copy-start(s32[16]{0:T(128)} %param.17) | copy-start | bytes 196
  66.4 28.3 %all-to-all-start.7 = ((f32[4,256,512]{2,1,0:T(8,128)}), f32[4,256,512]{2,1,0:T(8,128)S(1)}, u32[]{:S(2)}, u32[]{:S(2)}) async-start(f32[4,256,512]{2,1,0:T(8,128)} %stack.65), calls=%async_computation.7 | async-start | bytes 4194304 | tf_op jit(solution)/shard_map/all_to_all | solution.py:53
  71.5 5.5 %collective-permute-start = (f32[7,1024]{1,0:T(8,128)S(1)}, f32[7,1024]{1,0:T(8,128)S(1)}, u32[]{:S(2)}, u32[]{:S(2)}) collective-permute-start(f32[7,1024]{1,0:T(8,128)S(1)} %select_bitcast_fusion), channel_id=1, source_target_pairs={{0,1},{1,0},{2,3},{3,2},{4,5},{5,4},{6,7},{7,6},{8,9},{9,8},{10,11... | collective-permute-start | bytes 86024 | tf_op jit(solution)/shard_map/ppermute | solution.py:41
  94.8 1.4 copy-start.5
  97.9 10.2 %copy-start.16 = (s32[1,2,224]{2,1,0:T(2,128)S(1)}, s32[1,2,224]{2,1,0:T(2,128)}, u32[]{:S(2)}) copy-start(s32[1,2,224]{2,1,0:T(2,128)} %param.18) | copy-start | bytes 5380
  97.9 10.3 %copy-start.1 = (f32[64]{0:T(128)S(1)}, f32[64]{0:T(128)}, u32[]{:S(2)}) copy-start(f32[64]{0:T(128)} %param.20) | copy-start | bytes 772
  97.9 54.9 %all-to-all-start = ((f32[32,2,7,1024]{3,1,2,0:T(2,128)}), f32[32,2,7,1024]{3,1,2,0:T(2,128)S(1)}, u32[]{:S(2)}, u32[]{:S(2)}) async-start(f32[32,2,7,1024]{3,1,2,0:T(2,128)} %broadcast_in_dim.34), calls=%async_computation | async-start | bytes 3670016 | tf_op jit(solution)/shard_map/all_to_all | solution.py:44
  154.3 31.3 %all-to-all-start.1 = ((f32[4,256,512]{2,1,0:T(8,128)}), f32[4,256,512]{2,1,0:T(8,128)}, u32[]{:S(2)}, u32[]{:S(2)}) async-start(f32[4,256,512]{2,1,0:T(8,128)} %stack.59), calls=%async_computation.1 | async-start | bytes 4194304 | tf_op jit(solution)/shard_map/all_to_all | solution.py:53
  158.8 8.4 %copy-start.4 = (f32[4,256,512]{2,1,0:T(8,128)S(1)}, f32[4,256,512]{2,1,0:T(8,128)}, u32[]{:S(2)}) copy-start(f32[4,256,512]{2,1,0:T(8,128)} %copy-done.3) | copy-start | bytes 6291460
  165.1 56.3 %collective-permute-start.2 = (f32[32,7,512]{2,0,1:T(8,128)}, f32[32,7,512]{2,0,1:T(8,128)S(1)}, u32[]{:S(2)}, u32[]{:S(2)}) collective-permute-start(f32[32,7,512]{2,0,1:T(8,128)} %dynamic-slice_bitcast_fusion.2), channel_id=1, source_target_pairs={{0,1},{1,0},{2,3},{3,2},{4,5},{5,4},{6,7},{7,6},{8,9},{9,8},{10,11... | collective-permute-start | bytes 1376264 | tf_op jit(solution)/shard_map/ppermute | solution.py:64
  167.2 6.0 %copy-start.6 = (f32[4,256,512]{2,1,0:T(8,128)S(1)}, f32[4,256,512]{2,1,0:T(8,128)}, u32[]{:S(2)}) copy-start(f32[4,256,512]{2,1,0:T(8,128)} %copy-done.5) | copy-start | bytes 6291460
  170.8 6.0 %copy-start.7 = (f32[32,2,7,512]{3,0,2,1:T(8,128)}, f32[32,2,7,512]{3,0,2,1:T(8,128)S(1)}, u32[]{:S(2)}) copy-start(f32[32,2,7,512]{3,0,2,1:T(8,128)S(1)} %fusion.2) | copy-start | bytes 2752516
  171.8 49.6 %collective-permute-start.3 = (f32[32,7,512]{2,0,1:T(8,128)}, f32[32,7,512]{2,0,1:T(8,128)}, u32[]{:S(2)}, u32[]{:S(2)}) collective-permute-start(f32[32,7,512]{2,0,1:T(8,128)} %dynamic-slice_bitcast_fusion.1), channel_id=1, source_target_pairs={{0,1},{1,0},{2,3},{3,2},{4,5},{5,4},{6,7},{7,6},{8,9},{9,8},{10,11... | collective-permute-start | bytes 1376264 | tf_op jit(solution)/shard_map/ppermute | solution.py:64
  176.8 1.1 copy-start.9
  177.9 43.5 %collective-permute-start.4 = (f32[32,7,512]{2,0,1:T(8,128)}, f32[32,7,512]{2,0,1:T(8,128)}, u32[]{:S(2)}, u32[]{:S(2)}) collective-permute-start(f32[32,7,512]{2,0,1:T(8,128)} %dynamic-slice_bitcast_fusion), channel_id=1, source_target_pairs={{0,1},{1,0},{2,3},{3,2},{4,5},{5,4},{6,7},{7,6},{8,9},{9,8},{10,11... | collective-permute-start | bytes 1376264 | tf_op jit(solution)/shard_map/ppermute | solution.py:64
  190.9 0.9 copy-start.11
  192.6 28.8 %collective-permute-start.1 = (f32[32,7,512]{2,0,1:T(8,128)}, f32[32,7,512]{2,0,1:T(8,128)}, u32[]{:S(2)}, u32[]{:S(2)}) collective-permute-start(f32[32,7,512]{2,0,1:T(8,128)} %dynamic-slice_bitcast_fusion.3), channel_id=1, source_target_pairs={{0,1},{1,0},{2,3},{3,2},{4,5},{5,4},{6,7},{7,6},{8,9},{9,8},{10,11... | collective-permute-start | bytes 1376264 | tf_op jit(solution)/shard_map/ppermute | solution.py:64
  208.0 14.3 %copy-start.8 = (f32[32,2,7,512]{3,0,2,1:T(8,128)S(1)}, f32[32,2,7,512]{3,0,2,1:T(8,128)}, u32[]{:S(2)}) copy-start(f32[32,2,7,512]{3,0,2,1:T(8,128)} %copy-done.7) | copy-start | bytes 2752516
  208.0 14.3 %copy-start.10 = (f32[32,2,7,512]{3,0,2,1:T(8,128)S(1)}, f32[32,2,7,512]{3,0,2,1:T(8,128)}, u32[]{:S(2)}) copy-start(f32[32,2,7,512]{3,0,2,1:T(8,128)} %copy-done.9) | copy-start | bytes 2752516
  221.4 0.8 copy-start.14
  225.2 5.6 %copy-start.13 = (f32[32,7,512]{2,0,1:T(8,128)S(1)}, f32[32,7,512]{2,0,1:T(8,128)}, u32[]{:S(2)}) copy-start(f32[32,7,512]{2,0,1:T(8,128)} %get-tuple-element.26) | copy-start | bytes 1376260
  225.2 27.5 %copy-start.12 = (f32[32,7,512]{2,0,1:T(8,128)S(1)}, f32[32,7,512]{2,0,1:T(8,128)}, u32[]{:S(2)}) copy-start(f32[32,7,512]{2,0,1:T(8,128)} %get-tuple-element.25) | copy-start | bytes 1376260
  226.3 22.3 %all-to-all-start.2 = ((f32[32,7,512]{2,1,0:T(8,128)}), f32[32,7,512]{2,1,0:T(8,128)S(1)}, u32[]{:S(2)}, u32[]{:S(2)}) async-start(f32[32,7,512]{2,1,0:T(8,128)} %copy.45), calls=%async_computation.2 | async-start | bytes 1048576 | tf_op jit(solution)/shard_map/all_to_all | solution.py:66
  248.6 21.9 %all-to-all-start.4 = ((f32[32,7,512]{2,1,0:T(8,128)}), f32[32,7,512]{2,1,0:T(8,128)S(1)}, u32[]{:S(2)}, u32[]{:S(2)}) async-start(f32[32,7,512]{2,1,0:T(8,128)} %copy.47), calls=%async_computation.4 | async-start | bytes 1048576 | tf_op jit(solution)/shard_map/all_to_all | solution.py:66
  270.5 21.9 %all-to-all-start.6 = ((f32[32,7,512]{2,1,0:T(8,128)}), f32[32,7,512]{2,1,0:T(8,128)S(1)}, u32[]{:S(2)}, u32[]{:S(2)}) async-start(f32[32,7,512]{2,1,0:T(8,128)} %copy.49), calls=%async_computation.6 | async-start | bytes 1048576 | tf_op jit(solution)/shard_map/all_to_all | solution.py:66
